TPU v7x, 32 devices: a whole 2x2x4 slice. The times are simulated.
32 devices in a mesh: groups: 2 (over y), span: 4 (over z), layer: 2 (over x), rep: 2 (over core).
Axes of the slice: x: 2, y: 2, z: 4, core: 2. Of those that a mesh axis runs over, the one named last changes fastest.
Arguments:
- queries: bfloat16 [4096, 2, 4096], P('groups', 'layer', 'span'), parts along dimension 0, may hold values from -6 to 6
- train_grads: bfloat16 [4096, 2, 4096], P(('groups', 'span'), 'layer'), parts along dimension 0, may hold values from -6 to 6
- precond: float32 [2, 4096], P('layer', 'span'), may hold values from 0.25 to 4
- requests: int32 [8, 6], P('groups'), parts along dimension 0, may hold values from 0 to 15, as said below
- pair_slot: int32 [8, 24], P(('groups', 'span')), parts along dimension 0, may hold values from 0 to 5
- pair_train: int32 [8, 24], P(('groups', 'span')), parts along dimension 0, may hold values from 0 to 3
- pair_count: int32 [8, 2], P(('groups', 'span')), parts along dimension 0, may hold values from 1 to 12, as said below
Outputs:
- scores: float32 [8, 3072, 128], P(('groups', 'span'), ('layer', 'rep')), parts along dimension 0
There are 2 independent parts, one for each index of `groups`. A program takes and returns all parts, laid end to end along the dimension named above; an argument that names none is the same for every part. Nothing has to cross between parts.
Inputs may be any that keep to these rules, and one draw needn't show every extreme that they name: `requests`: each row names 6 different query blocks. The live pairs of half h of shard c's list are the first pair_count[c, h] of that half's 12 slots; some half is full in every draw.
All inputs are finite; a program needn't handle non-finite values.
Results may differ from a plain program's by a relative error of at most 0.0029.
Values may be sent and summed in bfloat16 or wider, within the bound.
No kernel may reach another device: no remote copies, remote signals or barrier semaphores. Data moves between devices by JAX's collectives and lax.ppermute only.
A program may use at most 64 MiB of HBM per device.

v0:
```python
import math

import jax
import jax.numpy as jnp
from jax import lax
from jax.sharding import PartitionSpec as P

D = 4096
L_DEV = 1
BLOCK = 128
NQ = 2048
PHALF = 12
TB_DEV = 4
PMAX = 24


def shards(queries, train_grads, precond, requests, pair_slot, pair_train, pair_count):
    features = queries.shape[2]
    prepared = (queries.astype(jnp.float32) * precond[None]).astype(jnp.bfloat16)
    query_blocks = prepared.reshape(NQ // BLOCK, BLOCK, L_DEV, features)
    rep_index = lax.axis_index("rep")
    picked = query_blocks[requests.reshape(-1)]
    arrived = lax.all_to_all(picked, "span", split_axis=0, concat_axis=3, tiled=True)
    score_scale = 1.0 / math.sqrt(L_DEV * lax.axis_size("layer") * D)
    train_blocks = train_grads.reshape(TB_DEV, BLOCK, L_DEV, D)
    slot_row = pair_slot[0]
    train_row = pair_train[0]
    counts = pair_count[0]
    partials = jnp.zeros((PMAX * BLOCK, BLOCK), jnp.float32)

    def score_into(slot_index, buffer):
        query_tile = arrived[slot_row[slot_index]]
        train_tile = train_blocks[train_row[slot_index]]
        partial_value = (
            lax.dot_general(
                query_tile,
                train_tile,
                (((1, 2), (1, 2)), ((), ())),
                preferred_element_type=jnp.float32,
            )
            * score_scale
        )
        return lax.dynamic_update_slice(buffer, partial_value, (slot_index * BLOCK, 0))

    first_slot = rep_index * PHALF

    def take_turn(turn, buffer):
        return score_into(first_slot + turn, buffer)

    partials = lax.fori_loop(0, counts[rep_index], take_turn, partials)
    summed = lax.psum_scatter(partials, ("layer", "rep"), scatter_dimension=0, tiled=True)
    return summed[None]


def solution(mesh):
    placed = (
        P("groups", "layer", "span"),
        P(("groups", "span"), "layer", None),
        P("layer", "span"),
        P("groups", None),
        P(("groups", "span"), None),
        P(("groups", "span"), None),
        P(("groups", "span"), None),
    )
    return jax.shard_map(
        shards,
        mesh=mesh,
        in_specs=placed,
        out_specs=P(("groups", "span"), ("layer", "rep"), None),
        check_vma=False,
    )
```

profile of v0, /device:TPU:0, one launch (start us, length us, event | category | flops | bytes accessed | tf_op | source)
XLA Modules:
  0.0 293.3 jit_solution(11145867026292086282)
XLA Ops:
  6.5 0.0 copy-start
  6.5 0.8 reshape.51
  7.3 5.4 %multiply_convert_fusion = bf16[2048,1,1024]{2,0,1:T(8,128)(2,1)} fusion(bf16[2048,1,1024]{2,0,1:T(8,128)(2,1)} %param.9, f32[1024]{0:T(1024)} %bitcast.37), kind=kLoop, calls=%fused_computation.8 | loop fusion | flops 6291456 | bytes 8392704 | tf_op jit(solution)/shard_map/convert_element_type | solution.py:19
  12.7 6.6 %gather_fusion = bf16[24,128,1024]{2,1,0:T(8,128)(2,1)} fusion(bf16[16,128,1024]{2,1,0:T(8,128)(2,1)} %bitcast.33, s32[1024]{0:T(1024)S(1)} %pad_clamp_fusion), kind=kCustom, calls=%fused_computation | custom fusion | bytes 12583008 | tf_op jit(solution)/shard_map/gather | solution.py:22
  19.3 6.3 %all-to-all-start = ((bf16[24,128,1,1024]{3,1,2,0:T(8,128)(2,1)}), bf16[24,128,1,1024]{3,1,2,0:T(8,128)(2,1)}, u32[]{:S(2)}, u32[]{:S(2)}) async-start(bf16[24,128,1,1024]{3,1,2,0:T(8,128)(2,1)} %bitcast.34), calls=%async_computation | async-start | bytes 12582912 | tf_op jit(solution)/shard_map/all_to_all | solution.py:23
  25.7 0.0 reduce-scatter.2.cloned.1.call-start
  25.7 0.0 copy-done
  25.7 0.6 constant_dynamic-slice_fusion
  26.3 138.2 %all-to-all-done = bf16[24,128,1,1024]{3,1,2,0:T(8,128)(2,1)} async-done(((bf16[24,128,1,1024]{3,1,2,0:T(8,128)(2,1)}), bf16[24,128,1,1024]{3,1,2,0:T(8,128)(2,1)}, u32[]{:S(2)}, u32[]{:S(2)}) %all-to-all-start) | async-done | bytes 6291488 | tf_op jit(solution)/shard_map/all_to_all | solution.py:23
  164.4 0.0 copy-start.2
  164.4 0.0 copy-start.3
  164.4 8.6 %copy.11 = bf16[6,128,1,4,1024]{1,4,3,0,2:T(8,128)(2,1)} copy(bf16[6,128,1,4,1024]{4,1,0,3,2:T(8,128)(2,1)} %bitcast.11) | data formatting | bytes 12582912 | tf_op jit(solution)/shard_map/all_to_all | solution.py:23
  173.1 0.1 broadcast_in_dim.8
  173.2 0.0 copy-done.2
  173.2 0.0 copy-done.3
  173.2 7.8 %while.10 = (s32[]{:T(128)}, f32[3072,128]{1,0:T(8,128)S(1)}, s32[]{:T(128)}, s32[]{:T(128)}, s32[24]{0:T(128)S(1)}, /*index=5*/bf16[6,128,1,4096]{1,3,0,2:T(8,1...) while((s32[]{:T(128)}, f32[3072,128]{1,0:T(8,128)S(1)}, ...), condition=%wide.region_1.0_spmd, body=%wide.region_0.0_spmd.sunk | while | flops 134234128 | bytes 2163025 | solution.py:50
  173.8 0.6 dynamic_slice.32
  176.1 0.6 dynamic_slice.31
  178.3 2.0 fusion.12
  181.0 0.0 copy-start.1
  181.0 1.1 copy-done.1
  182.1 0.0 reduce-scatter.2.cloned.1.call-update
  182.1 104.4 %reduce-scatter.2.cloned.1.call-done = f32[768,128]{1,0:T(8,128)} async-done(((f32[3072,128]{1,0:T(8,128)}), f32[768,128]{1,0:T(8,128)}) %reduce-scatter.2.cloned.1.call-update) | async-done | bytes 393232 | tf_op jit(solution)/shard_map/reduce_scatter | solution.py:51
  (2 shorter events, 0.0 us)
Async XLA Ops:
  6.5 19.1 %copy-start = (s32[1,2]{1,0:T(1,128)S(1)}, s32[1,2]{1,0:T(1,128)}, u32[]{:S(2)}) copy-start(s32[1,2]{1,0:T(1,128)} %param.15) | copy-start | bytes 28
  19.3 145.1 %all-to-all-start = ((bf16[24,128,1,1024]{3,1,2,0:T(8,128)(2,1)}), bf16[24,128,1,1024]{3,1,2,0:T(8,128)(2,1)}, u32[]{:S(2)}, u32[]{:S(2)}) async-start(bf16[24,128,1,1024]{3,1,2,0:T(8,128)(2,1)} %bitcast.34), calls=%async_computation | async-start | bytes 12582912 | tf_op jit(solution)/shard_map/all_to_all | solution.py:23
  25.7 260.8 %reduce-scatter.2.cloned.1.call-start = ((), (), s32[]{:S(2)}) async-start(), calls=%async_computation.2 | async-start | bytes 1966080 | tf_op jit(solution)/shard_map/reduce_scatter | solution.py:51
  164.4 8.7 %copy-start.2 = (s32[1,24]{1,0:T(1,128)S(1)}, s32[1,24]{1,0:T(1,128)}, u32[]{:S(2)}) copy-start(s32[1,24]{1,0:T(1,128)} %param.13) | copy-start | bytes 292
  164.4 8.7 %copy-start.3 = (s32[1,24]{1,0:T(1,128)S(1)}, s32[1,24]{1,0:T(1,128)}, u32[]{:S(2)}) copy-start(s32[1,24]{1,0:T(1,128)} %param.14) | copy-start | bytes 292
  181.0 1.1 copy-start.1
Sparse Core Ops, SparseCore 0:
  182.3 104.1 reduce-scatter.1
where the time goes:
time: 295 us; the launch traced here: 293 us
  waiting for transfers between devices  243 us (82%)
  local copies, waits for them, and re-layouts  19 us (6%)
  between operations  13.4 us (5%)
  starting transfers between devices  6.35 us (2%)
  other arithmetic  5.38 us (2%)
  loops' own time  4.62 us (2%)
    all_to_all x1, waiting for transfers between devices, shards(): lax.all_to_all(picked, 'span', split_axis=0, concat_axis=3, tiled=True)  138 us
    reduce_scatter x1, waiting for transfers between devices, shards(): lax.psum_scatter(partials, ('layer', 'rep'), scatter_dimension=0, tiled=T...  104 us
    all_to_all x1, local copies, waits for them, and re-layouts, shards(): lax.all_to_all(picked, 'span', split_axis=0, concat_axis=3, tiled=True)  8.63 us
    gather x1, local copies, waits for them, and re-layouts, shards(): picked = query_blocks[requests.reshape(-1)]  6.62 us
    all_to_all x1, starting transfers between devices, shards(): lax.all_to_all(picked, 'span', split_axis=0, concat_axis=3, tiled=True)  6.35 us
  transfers between devices with their start and end apart: 2, of which 2 were waited for; matrix products, arithmetic and copies ran while one was open for 0% of the time, Pallas kernels for 0%

commit v1 on v0

v1 whole, which is shorter than its diff:
```python
import math

import jax
import jax.numpy as jnp
from jax import lax
from jax.sharding import PartitionSpec as P

BLOCK = 128


def shards(queries, train_grads, precond, requests, pair_slot, pair_train, pair_count):
    n_query, l_dev, features = queries.shape
    n_span = lax.axis_size("span")
    n_rep = lax.axis_size("rep")
    d_full = train_grads.shape[2]
    tb_dev = train_grads.shape[0] // BLOCK
    pmax = pair_slot.shape[1]
    cap = requests.shape[1]
    phalf = pmax // pair_count.shape[1]
    half = features // n_rep
    rep_index = lax.axis_index("rep")

    q_half = lax.dynamic_slice_in_dim(queries, rep_index * half, half, axis=2)
    p_half = lax.dynamic_slice_in_dim(precond, rep_index * half, half, axis=1)
    q_blocks = q_half.reshape(n_query // BLOCK, BLOCK, l_dev, half)
    picked = q_blocks[requests.reshape(-1)]
    picked = (picked.astype(jnp.float32) * p_half[None, None]).astype(jnp.bfloat16)
    picked = picked.reshape(n_span, cap, BLOCK, l_dev, half)
    arrived = lax.all_to_all(picked, "span", split_axis=0, concat_axis=0, tiled=True)

    train = train_grads.reshape(tb_dev, BLOCK, l_dev, n_span, n_rep, half)
    train = lax.dynamic_index_in_dim(train, rep_index, axis=4, keepdims=False)

    combos = lax.dot_general(
        arrived,
        train,
        (((0, 3, 4), (3, 2, 4)), ((), ())),
        preferred_element_type=jnp.float32,
    )
    score_scale = 1.0 / math.sqrt(l_dev * lax.axis_size("layer") * d_full)
    combos = jnp.transpose(combos, (0, 2, 1, 3)).reshape(cap * tb_dev, BLOCK, BLOCK)
    slot_row = pair_slot[0]
    train_row = pair_train[0]
    counts = pair_count[0]
    chosen = combos[slot_row * tb_dev + train_row] * score_scale
    slots = jnp.arange(pmax, dtype=jnp.int32)
    live = (slots % phalf) < counts[slots // phalf]
    partials = jnp.where(live[:, None, None], chosen, 0.0).reshape(pmax * BLOCK, BLOCK)
    summed = lax.psum_scatter(partials, ("layer", "rep"), scatter_dimension=0, tiled=True)
    return summed[None]


def solution(mesh):
    placed = (
        P("groups", "layer", "span"),
        P(("groups", "span"), "layer", None),
        P("layer", "span"),
        P("groups", None),
        P(("groups", "span"), None),
        P(("groups", "span"), None),
        P(("groups", "span"), None),
    )
    return jax.shard_map(
        shards,
        mesh=mesh,
        in_specs=placed,
        out_specs=P(("groups", "span"), ("layer", "rep"), None),
        check_vma=False,
    )
```

time: 295 us -> 138 us (0.47)
  waiting for transfers between devices: 243 us -> 79.6 us
  local copies, waits for them, and re-layouts: 19 us -> 24 us
  loops' own time: 4.62 us -> 0 us
  matrix products: 2.03 us -> 5.32 us
    all_to_all x1, waiting for transfers between devices: 138 us -> 52.4 us  [shards(): lax.all_to_all(picked, 'span', split_axis=0, concat_axis=0, tiled=True)]
    reduce_scatter x1, waiting for transfers between devices: 104 us -> 27.3 us  [shards(): lax.psum_scatter(partials, ('layer', 'rep'), scatter_dimension=0, tiled=T...]
    all_to_all x1 -> x0, local copies, waits for them, and re-layouts: 8.63 us -> none  [shards(): lax.all_to_all(picked, 'span', split_axis=0, concat_axis=3, tiled=True)]
    dynamic_slice x3, local copies, waits for them, and re-layouts: 1.73 us -> 10.2 us  [the longest x1 8.49 us: shards(): train = lax.dynamic_index_in_dim(train, rep_index, axis=4, keepdims=False)]
    reshape x1 -> x2, local copies, waits for them, and re-layouts: 0.78 us -> 8.57 us  [the longest x1 7.8 us: shards(): train = train_grads.reshape(tb_dev, BLOCK, l_dev, n_span, n_rep, half)]
    another operation x1 -> x0, loops' own time: 4.62 us -> none  [shards(): partials = lax.fori_loop(0, counts[rep_index], take_turn, partials)]
    dot_general x1, matrix products: 2.03 us -> 5.32 us  [shards(): lax.dot_general(arrived, train, (((0, 3, 4), (3, 2, 4)), ((), ())), prefe...]
    gather x1 -> x3, local copies, waits for them, and re-layouts: 6.62 us -> 5.13 us  [the longest x1 2.5 us: shards(): picked = q_blocks[requests.reshape(-1)]]
  transfers between devices with their start and end apart: 2 -> 2, of which waited for: 2 -> 2; matrix products, arithmetic and copies ran while one was open for 0% -> 13% of each run, Pallas kernels for 0% -> 0%
where the time goes in v1:
time: 138 us; the launch traced here: 137 us
  waiting for transfers between devices  79.6 us (58%)
  local copies, waits for them, and re-layouts  24 us (17%)
  between operations  13.5 us (10%)
  other arithmetic  8.32 us (6%)
  starting transfers between devices  6.35 us (5%)
  matrix products  5.32 us (4%)
    all_to_all x1, waiting for transfers between devices, shards(): lax.all_to_all(picked, 'span', split_axis=0, concat_axis=0, tiled=True)  52.4 us
    reduce_scatter x1, waiting for transfers between devices, shards(): lax.psum_scatter(partials, ('layer', 'rep'), scatter_dimension=0, tiled=T...  27.3 us
    dynamic_slice x1, local copies, waits for them, and re-layouts, shards(): train = lax.dynamic_index_in_dim(train, rep_index, axis=4, keepdims=False)  8.49 us
    reshape x1, local copies, waits for them, and re-layouts, shards(): train = train_grads.reshape(tb_dev, BLOCK, l_dev, n_span, n_rep, half)  7.8 us
    all_to_all x1, starting transfers between devices, shards(): lax.all_to_all(picked, 'span', split_axis=0, concat_axis=0, tiled=True)  6.35 us
    dot_general x1, matrix products, shards(): lax.dot_general(arrived, train, (((0, 3, 4), (3, 2, 4)), ((), ())), prefe...  5.32 us
    convert_element_type x1, other arithmetic, shards(): (picked.astype(jnp.float32) * p_half[None, None]).astype(jnp.bfloat16)  4.34 us
  transfers between devices with their start and end apart: 2, of which 2 were waited for; matrix products, arithmetic and copies ran while one was open for 13% of the time, Pallas kernels for 0%

profile of v1, /device:TPU:0, one launch (start us, length us, event | category | flops | bytes accessed | tf_op | source)
XLA Modules:
  0.0 137.1 jit_solution(10960529995080273040)
XLA Ops:
  6.5 0.0 copy-start
  6.5 0.8 reshape.166
  7.3 1.7 %constant_dynamic-slice_fusion.2 = bf16[2048,1,512]{2,0,1:T(8,128)(2,1)S(1)} fusion(bf16[2048,1,1024]{2,0,1:T(8,128)(2,1)} %param.7, s32[]{:T(128)S(6)} %select_n.69), kind=kLoop, calls=%fused_computation.25 | loop fusion | bytes 4194308 | tf_op jit(solution)/shard_map/dynamic_slice | solution.py:23
  9.1 0.0 copy-done
  9.1 2.5 %gather_fusion = bf16[24,128,512]{2,1,0:T(8,128)(2,1)} fusion(bf16[16,128,512]{2,1,0:T(8,128)(2,1)S(1)} %bitcast.42, s32[1024]{0:T(1024)S(1)} %pad_clamp_fusion.1), kind=kCustom, calls=%fused_computation | custom fusion | bytes 6291552 | tf_op jit(solution)/shard_map/gather | solution.py:26
  11.6 4.3 %fusion.1 = bf16[4,6,128,1,512]{4,2,1,3,0:T(8,128)(2,1)} fusion(bf16[4,6,128,1,512]{4,2,1,0,3:T(8,128)(2,1)} %bitcast.43, f32[512]{0:T(512)S(1)} %bitcast.45), kind=kLoop, calls=%fused_computation.4 | loop fusion | flops 4718592 | bytes 6293504 | tf_op jit(solution)/shard_map/convert_element_type | solution.py:27
  15.9 6.3 %all-to-all-start = ((bf16[4,6,128,1,512]{4,2,1,3,0:T(8,128)(2,1)}), bf16[4,6,128,1,512]{4,2,1,3,0:T(8,128)(2,1)S(1)}, u32[]{:S(2)}, u32[]{:S(2)}) async-start(bf16[4,6,128,1,512]{4,2,1,3,0:T(8,128)(2,1)} %fusion.1), calls=%async_computation | async-start | bytes 6291456 | tf_op jit(solution)/shard_map/all_to_all | solution.py:29
  22.3 0.0 reduce-scatter.2.cloned.1.call-start
  22.3 0.0 copy-start.1
  22.3 0.0 copy-start.2
  22.3 0.0 copy-start.3
  22.3 7.8 %reshape.168 = bf16[4,128,1,4,2,512]{5,4,3,1,0,2:T(2,128)(2,1)} reshape(bf16[512,1,4096]{2,0,1:T(8,128)(2,1)} %param.8) | data formatting | bytes 8388608 | tf_op jit(solution)/shard_map/reshape | solution.py:31
  30.1 0.0 copy-done.1
  30.1 0.6 fusion.9
  30.7 1.3 fusion.5
  32.0 0.0 copy-done.2
  32.0 0.0 copy-done.3
  32.0 0.1 broadcast_bitcast_fusion
  32.1 8.5 %constant_dynamic-slice_fusion = bf16[4,128,1,4,1,512]{5,4,3,1,0,2:T(2,128)(2,1)} fusion(bf16[4,128,1,4,2,512]{5,4,3,1,0,2:T(2,128)(2,1)} %reshape.168, s32[]{:T(128)S(6)} %select_n.71), kind=kLoop, calls=%fused_computation.23 | loop fusion | bytes 4194308 | tf_op jit(solution)/shard_map/jit(dynamic_index_in_dim)/dynamic_slice | solution.py:32
  40.6 52.4 %all-to-all-done = bf16[4,6,128,1,512]{4,2,1,3,0:T(8,128)(2,1)S(1)} async-done(((bf16[4,6,128,1,512]{4,2,1,3,0:T(8,128)(2,1)}), bf16[4,6,128,1,512]{4,2,1,3,0:T(8,128)(2,1)S(1)}, u32[]{:S(2)}, u32[]{:S(2)}) %all-to-all-start) | async-done | bytes 3145760 | tf_op jit(solution)/shard_map/all_to_all | solution.py:29
  92.9 5.3 %fusion.2 = f32[6,128,4,128,1]{3,1,4,2,0:T(8,128)} fusion(bf16[4,6,128,1,512]{4,2,1,3,0:T(8,128)(2,1)S(1)} %all-to-all-done, bf16[4,128,1,4,1,512]{5,4,3,1,0,2:T(2,128)(2,1)} %constant_dynamic-slice_fusion), kind=kOutput, calls=%fused_computation.5 | convolution fusion | flops 1610612736 | bytes 6815744 | tf_op jit(solution)/shard_map/dot_general | solution.py:34
  98.3 2.1 %gather_fusion.1 = f32[24,128,128]{2,1,0:T(8,128)S(1)} fusion(f32[24,128,128]{2,1,0:T(8,128)} %bitcast.44, s32[1024]{0:T(1024)S(1)} %pad_clamp_fusion), kind=kCustom, calls=%fused_computation.1 | custom fusion | bytes 3145824 | tf_op jit(solution)/shard_map/gather | solution.py:45
  100.3 0.2 broadcast_multiply_fusion
  100.5 2.5 %bitcast_select_fusion = f32[3072,128]{1,0:T(8,128)} fusion(f32[24,128,128]{2,1,0:T(8,128)S(1)} %broadcast_multiply_fusion, pred[3072]{0:T(1024)(128)(4,1)S(1)} %broadcast_bitcast_fusion), kind=kLoop, calls=%fused_computation.9 | loop fusion | flops 393216 | bytes 3148800 | tf_op jit(solution)/shard_map/jit(_where)/select_n | solution.py:48
  103.0 0.0 reduce-scatter.2.cloned.1.call-update
  103.0 27.3 %reduce-scatter.2.cloned.1.call-done = f32[768,128]{1,0:T(8,128)} async-done(((f32[3072,128]{1,0:T(8,128)}), f32[768,128]{1,0:T(8,128)}) %reduce-scatter.2.cloned.1.call-update) | async-done | bytes 393232 | tf_op jit(solution)/shard_map/reduce_scatter | solution.py:49
  (5 shorter events, 0.0 us)
Async XLA Ops:
  6.5 2.5 %copy-start = (f32[1,1024]{1,0:T(1,128)S(1)}, f32[1,1024]{1,0:T(1,128)}, u32[]{:S(2)}) copy-start(f32[1,1024]{1,0:T(1,128)} %param.9) | copy-start | bytes 12292
  15.9 77.0 %all-to-all-start = ((bf16[4,6,128,1,512]{4,2,1,3,0:T(8,128)(2,1)}), bf16[4,6,128,1,512]{4,2,1,3,0:T(8,128)(2,1)S(1)}, u32[]{:S(2)}, u32[]{:S(2)}) async-start(bf16[4,6,128,1,512]{4,2,1,3,0:T(8,128)(2,1)} %fusion.1), calls=%async_computation | async-start | bytes 6291456 | tf_op jit(solution)/shard_map/all_to_all | solution.py:29
  22.3 108.0 %reduce-scatter.2.cloned.1.call-start = ((), (), s32[]{:S(2)}) async-start(), calls=%async_computation.2 | async-start | bytes 1966080 | tf_op jit(solution)/shard_map/reduce_scatter | solution.py:49
  22.3 7.8 %copy-start.1 = (s32[1,2]{1,0:T(1,128)S(1)}, s32[1,2]{1,0:T(1,128)}, u32[]{:S(2)}) copy-start(s32[1,2]{1,0:T(1,128)} %param.13) | copy-start | bytes 28
  22.3 9.7 %copy-start.2 = (s32[1,24]{1,0:T(1,128)S(1)}, s32[1,24]{1,0:T(1,128)}, u32[]{:S(2)}) copy-start(s32[1,24]{1,0:T(1,128)} %param.12) | copy-start | bytes 292
  22.3 9.7 %copy-start.3 = (s32[1,24]{1,0:T(1,128)S(1)}, s32[1,24]{1,0:T(1,128)}, u32[]{:S(2)}) copy-start(s32[1,24]{1,0:T(1,128)} %param.11) | copy-start | bytes 292
Sparse Core Ops, SparseCore 0:
  103.2 27.0 reduce-scatter.1

commit v2 on v1

v2 whole, which is shorter than its diff:
```python
import math

import jax
import jax.numpy as jnp
from jax import lax
from jax.sharding import PartitionSpec as P

BLOCK = 128
ROW_CHUNKS = 2


def ring_reduce_scatter(x, axis_name, dim):
    n = lax.axis_size(axis_name)
    me = lax.axis_index(axis_name)

    def piece(c):
        return lax.dynamic_index_in_dim(x, c % n, axis=dim, keepdims=False)

    if n == 1:
        return piece(me)
    perm = [(i, (i + 1) % n) for i in range(n)]
    acc = piece(me - 1 + n)
    for t in range(n - 1):
        recv = lax.ppermute(acc, axis_name, perm)
        acc = recv + piece(me - 2 - t + 2 * n)
    return acc


def shards(queries, train_grads, precond, requests, pair_slot, pair_train, pair_count):
    n_query, l_dev, features = queries.shape
    n_span = lax.axis_size("span")
    n_rep = lax.axis_size("rep")
    n_layer = lax.axis_size("layer")
    d_full = train_grads.shape[2]
    tb_dev = train_grads.shape[0] // BLOCK
    pmax = pair_slot.shape[1]
    cap = requests.shape[1]
    phalf = pmax // pair_count.shape[1]
    half = features // n_rep
    per_dev = pmax // (n_layer * n_rep)
    rep_index = lax.axis_index("rep")
    span_index = lax.axis_index("span")
    rows = BLOCK // ROW_CHUNKS
    lh = l_dev * half

    q5 = queries.reshape(n_query // BLOCK, BLOCK, l_dev, n_rep, half)
    p_half = lax.dynamic_index_in_dim(
        precond.reshape(l_dev, n_rep, half), rep_index, axis=1, keepdims=False
    ).reshape(lh)
    train = train_grads.reshape(tb_dev * BLOCK, l_dev, n_span, n_rep, half)
    train = lax.dynamic_index_in_dim(train, rep_index, axis=3, keepdims=False)
    train = jnp.transpose(train, (0, 2, 1, 3)).reshape(tb_dev * BLOCK, n_span, lh)
    sources = (span_index - jnp.arange(n_span, dtype=jnp.int32) + n_span) % n_span
    train = jnp.take(train, sources, axis=1)
    train = jnp.concatenate([train, jnp.zeros((BLOCK, n_span, lh), train.dtype)], axis=0)

    score_scale = 1.0 / math.sqrt(l_dev * n_layer * d_full)
    slot_row = pair_slot[0]
    train_row = pair_train[0]
    counts = pair_count[0]
    slots = jnp.arange(pmax, dtype=jnp.int32)
    live = (slots % phalf) < counts[slots // phalf]
    pick_train = jnp.where(live, train_row, tb_dev)

    def prepared_piece(dest, chunk):
        req_row = requests[dest]
        got = q5[req_row, chunk * rows:(chunk + 1) * rows, :, rep_index, :]
        got = (got.reshape(cap, rows, lh).astype(jnp.float32) * p_half).astype(jnp.bfloat16)
        return got

    outs = []
    for chunk in range(ROW_CHUNKS):
        pieces = [prepared_piece(span_index, chunk)]
        for k in range(1, n_span):
            dest = (span_index + k) % n_span
            perm = [(i, (i + k) % n_span) for i in range(n_span)]
            pieces.append(lax.ppermute(prepared_piece(dest, chunk), "span", perm))
        arrived = jnp.stack(pieces, axis=0)
        combos = lax.dot_general(
            arrived,
            train,
            (((0, 3), (1, 2)), ((), ())),
            preferred_element_type=jnp.float32,
        ).reshape(cap, rows, tb_dev + 1, BLOCK)
        partial = combos.at[slot_row, :, pick_train, :].get(mode="promise_in_bounds") * score_scale
        partial = partial.reshape(n_layer, n_rep, per_dev, rows, BLOCK)
        partial = ring_reduce_scatter(partial, "rep", 1)
        partial = ring_reduce_scatter(partial, "layer", 0)
        outs.append(partial)
    summed = jnp.concatenate(outs, axis=1).reshape(per_dev * BLOCK, BLOCK)
    return summed[None]


def solution(mesh):
    placed = (
        P("groups", "layer", "span"),
        P(("groups", "span"), "layer", None),
        P("layer", "span"),
        P("groups", None),
        P(("groups", "span"), None),
        P(("groups", "span"), None),
        P(("groups", "span"), None),
    )
    return jax.shard_map(
        shards,
        mesh=mesh,
        in_specs=placed,
        out_specs=P(("groups", "span"), ("layer", "rep"), None),
        check_vma=False,
    )
```

time: 138 us -> 127 us (0.920)
  the two profiles are of different devices: /device:TPU:0 before, /device:TPU:10 now
where the time goes in v2:
time: 127 us
  local copies, waits for them, and re-layouts  56.1 us (44%)
  waiting for transfers between devices  44.5 us (35%)
  starting transfers between devices  11.1 us (9%)
  other arithmetic  8.59 us (7%)
  matrix products  6.04 us (5%)
    ppermute x6, waiting for transfers between devices, shards(): pieces.append(lax.ppermute(prepared_piece(dest, chunk), 'span', perm))  34.4 us
    gather x8, local copies, waits for them, and re-layouts, prepared_piece(): got = q5[req_row, chunk * rows:(chunk + 1) * rows, :, rep_index, :]  21.3 us
    reshape x2, local copies, waits for them, and re-layouts, shards(): q5 = queries.reshape(n_query // BLOCK, BLOCK, l_dev, n_rep, half)  16.7 us
    ppermute x4, waiting for transfers between devices, ring_reduce_scatter(): recv = lax.ppermute(acc, axis_name, perm)  10.2 us
    ppermute x6, starting transfers between devices, shards(): pieces.append(lax.ppermute(prepared_piece(dest, chunk), 'span', perm))  8.38 us
    unnamed x16, local copies, waits for them, and re-layouts  7 us
    dot_general x2, matrix products, shards(): lax.dot_general(arrived, train, (((0, 3), (1, 2)), ((), ())), preferred_e...  6.04 us
    dynamic_slice x2, local copies, waits for them, and re-layouts, shards(): train = lax.dynamic_index_in_dim(train, rep_index, axis=3, keepdims=False)  5.87 us
  transfers between devices with their start and end apart: 10, of which 8 were waited for; matrix products, arithmetic and copies ran while one was open for 22% of the time, Pallas kernels for 0%

profile of v2, /device:TPU:10, one launch (start us, length us, event | category | flops | bytes accessed | tf_op | source)
XLA Modules:
  0.0 126.6 jit_solution(2157576635802702725)
XLA Ops:
  0.0 0.5 broadcast.693
  0.5 1.3 %reduce.3 = f32[1024]{0:T(1024)S(1)} reduce(f32[1,1024]{1,0:T(1,128)} %param.9, f32[]{:T(128)} %broadcast.693), dimensions={0}, to_apply=%param.9.reduce_sub_computation.3 | reduce | bytes 8196 | tf_op args[2]
  1.9 7.9 %reshape.506 = bf16[16,128,2,512]{3,2,1,0:T(2,128)(2,1)} reshape(bf16[2048,1,1024]{2,0,1:T(8,128)(2,1)} %param.7) | data formatting | bytes 8388608 | tf_op jit(solution)/shard_map/reshape | solution.py:46
  9.8 0.0 copy-start.3
  9.8 8.9 %copy.44 = bf16[16,128,2,512]{3,2,0,1:T(2,128)(2,1)} copy(bf16[16,128,2,512]{3,2,1,0:T(2,128)(2,1)} %reshape.506) | data formatting | bytes 8388608 | tf_op jit(solution)/shard_map/reshape | solution.py:46
  18.6 0.0 copy-done.3
  18.7 2.7 %gather_fusion.9 = bf16[6,64,512]{2,0,1:T(8,128)(2,1)S(1)} fusion(bf16[16,128,2,512]{3,2,0,1:T(2,128)(2,1)} %copy.44, s32[6]{0:T(128)S(1)} %get-tuple-element.25), kind=kCustom, calls=%fused_computation.9 | custom fusion | bytes 786504 | tf_op jit(solution)/shard_map/gather | solution.py:67
  21.3 2.7 %gather_fusion.8 = bf16[6,64,512]{2,0,1:T(8,128)(2,1)S(1)} fusion(bf16[16,128,2,512]{3,2,0,1:T(2,128)(2,1)} %copy.44, s32[6]{0:T(128)S(1)} %get-tuple-element.23), kind=kCustom, calls=%fused_computation.8 | custom fusion | bytes 786504 | tf_op jit(solution)/shard_map/gather | solution.py:67
  24.0 2.7 %gather_fusion.7 = bf16[6,64,512]{2,0,1:T(8,128)(2,1)S(1)} fusion(bf16[16,128,2,512]{3,2,0,1:T(2,128)(2,1)} %copy.44, s32[6]{0:T(128)S(1)} %get-tuple-element.21), kind=kCustom, calls=%fused_computation.7 | custom fusion | bytes 786504 | tf_op jit(solution)/shard_map/gather | solution.py:67
  26.7 2.7 %gather_fusion.3 = bf16[6,64,512]{2,0,1:T(8,128)(2,1)S(1)} fusion(bf16[16,128,2,512]{3,2,0,1:T(2,128)(2,1)} %copy.44, s32[6]{0:T(128)S(1)} %bitcast.127), kind=kCustom, calls=%fused_computation.3 | custom fusion | bytes 786504 | tf_op jit(solution)/shard_map/gather | solution.py:67
  29.3 2.7 %gather_fusion.2 = bf16[6,64,512]{2,0,1:T(8,128)(2,1)S(1)} fusion(bf16[16,128,2,512]{3,2,0,1:T(2,128)(2,1)} %copy.44, s32[6]{0:T(128)S(1)} %bitcast.126), kind=kCustom, calls=%fused_computation.2 | custom fusion | bytes 786504 | tf_op jit(solution)/shard_map/gather | solution.py:67
  32.0 2.7 %gather_fusion.1 = bf16[6,64,512]{2,0,1:T(8,128)(2,1)S(1)} fusion(bf16[16,128,2,512]{3,2,0,1:T(2,128)(2,1)} %copy.44, s32[6]{0:T(128)S(1)} %bitcast.125), kind=kCustom, calls=%fused_computation.1 | custom fusion | bytes 786504 | tf_op jit(solution)/shard_map/gather | solution.py:67
  34.7 0.0 copy-start.4
  34.7 1.8 %fusion.37 = (bf16[6,64,512]{2,1,0:T(8,128)(2,1)}, bf16[6,64,512]{2,1,0:T(8,128)(2,1)}, bf16[6,64,512]{2,1,0:T(8,128)(2,1)}, bf16[6,64,512]{2,1,0:T(8,128)(2,1)}...) fusion(bf16[6,64,512]{2,0,1:T(8,128)(2,1)S(1)} %gather_fusion.1, f32[512]{0:T(512)S(1)} %bitcast.128, ...), kind=kLoop, calls=%fused_computation.51 | loop fusion | flops 3538944 | bytes 4720640 | tf_op jit(solution)/shard_map/convert_element_type | solution.py:68
  36.5 1.6 %collective-permute-start = (bf16[6,64,512]{2,1,0:T(8,128)(2,1)}, bf16[6,64,512]{2,1,0:T(8,128)(2,1)}, u32[]{:S(2)}, u32[]{:S(2)}) collective-permute-start(bf16[6,64,512]{2,1,0:T(8,128)(2,1)} %get-tuple-element.15), channel_id=1, source_target_pairs={{0,4},{4,8},{8,12},{12,0},{1,5},{5,9},{9,13},{13,1},{2,6},{6,10},{... | collective-permute-start | bytes 1179656 | tf_op jit(solution)/shard_map/ppermute | solution.py:77
  38.1 1.2 collective-permute-start.1
  39.3 1.8 %collective-permute-start.2 = (bf16[6,64,512]{2,1,0:T(8,128)(2,1)}, bf16[6,64,512]{2,1,0:T(8,128)(2,1)}, u32[]{:S(2)}, u32[]{:S(2)}) collective-permute-start(bf16[6,64,512]{2,1,0:T(8,128)(2,1)} %get-tuple-element.17), channel_id=1, source_target_pairs={{0,12},{4,0},{8,4},{12,8},{1,13},{5,1},{9,5},{13,9},{2,14},{6,2},{... | collective-permute-start | bytes 1179656 | tf_op jit(solution)/shard_map/ppermute | solution.py:77
  41.1 0.2 collective-permute-start.5
  41.3 3.5 %collective-permute-start.6 = (bf16[6,64,512]{2,1,0:T(8,128)(2,1)}, bf16[6,64,512]{2,1,0:T(8,128)(2,1)}, u32[]{:S(2)}, u32[]{:S(2)}) collective-permute-start(bf16[6,64,512]{2,1,0:T(8,128)(2,1)} %get-tuple-element.19), channel_id=1, source_target_pairs={{0,8},{4,12},{8,0},{12,4},{1,9},{5,13},{9,1},{13,5},{2,10},{6,14},... | collective-permute-start | bytes 1179656 | tf_op jit(solution)/shard_map/ppermute | solution.py:77
  44.8 0.0 copy-done.4
  44.8 0.6 fusion.72
  45.5 2.7 %gather_fusion.6 = bf16[6,64,512]{2,0,1:T(8,128)(2,1)S(1)} fusion(bf16[16,128,2,512]{3,2,0,1:T(2,128)(2,1)} %copy.44, s32[6]{0:T(128)S(1)} %get-tuple-element.5), kind=kCustom, calls=%fused_computation.6 | custom fusion | bytes 786504 | tf_op jit(solution)/shard_map/gather | solution.py:67
  48.1 2.7 %gather_fusion = bf16[6,64,512]{2,0,1:T(8,128)(2,1)S(1)} fusion(bf16[16,128,2,512]{3,2,0,1:T(2,128)(2,1)} %copy.44, s32[6]{0:T(128)S(1)} %bitcast.124), kind=kCustom, calls=%fused_computation | custom fusion | bytes 786504 | tf_op jit(solution)/shard_map/gather | solution.py:67
  50.8 6.5 %copy.55 = bf16[512,1,4096]{0,2,1:T(8,128)(2,1)} copy(bf16[512,1,4096]{2,0,1:T(8,128)(2,1)} %param.8) | data formatting | bytes 8388608 | tf_op args[1]
  57.3 3.1 %constant_dynamic-slice_fusion = bf16[512,1,4,1,512]{0,4,3,2,1:T(8,128)(2,1)} fusion(bf16[512,1,4,2,512]{0,4,3,2,1:T(8,128)(2,1)} %bitcast.116, s32[]{:T(128)S(6)} %select_n.244), kind=kLoop, calls=%fused_computation.65 | loop fusion | bytes 4194308 | tf_op jit(solution)/shard_map/jit(dynamic_index_in_dim)/dynamic_slice | solution.py:51
  60.4 2.8 %copy.56 = bf16[512,1,4,1,512]{4,0,3,2,1:T(8,128)(2,1)S(1)} copy(bf16[512,1,4,1,512]{0,4,3,2,1:T(8,128)(2,1)} %constant_dynamic-slice_fusion) | data formatting | bytes 4194304 | tf_op jit(solution)/shard_map/jit(dynamic_index_in_dim)/dynamic_slice | solution.py:51
  63.2 1.1 fusion.38
  64.3 2.0 %gather_fusion.4 = bf16[4,512,512]{2,1,0:T(8,128)(2,1)} fusion(bf16[512,4,512]{2,0,1:T(8,128)(2,1)S(1)} %bitcast.117, s32[1024]{0:T(1024)S(1)} %pad_clamp_fusion), kind=kCustom, calls=%fused_computation.4 | custom fusion | bytes 4194320 | tf_op jit(solution)/shard_map/jit(_take)/gather | solution.py:54
  66.3 0.0 copy-done.5
  66.3 0.0 copy-done.6
  66.3 1.2 fusion.63
  67.6 0.0 copy-start.2
  67.6 1.9 %select_bitcast_fusion = bf16[512,4,512]{2,0,1:T(8,128)(2,1)S(1)} fusion(bf16[4,512,512]{2,1,0:T(8,128)(2,1)} %gather_fusion.4, pred[4]{0:T(512)(128)(4,1)S(1)} %compare_and_fusion), kind=kLoop, calls=%fused_computation.17 | loop fusion | flops 1048576 | bytes 4194308 | tf_op jit(solution)/shard_map/jit(_take)/select_n | solution.py:54
  69.5 0.0 copy-start
  69.5 0.0 collective-permute-done
  69.5 0.1 collective-permute-start.7
  69.6 20.5 %collective-permute-done.1 = bf16[6,64,512]{2,1,0:T(8,128)(2,1)} collective-permute-done((bf16[6,64,512]{2,1,0:T(8,128)(2,1)}, bf16[6,64,512]{2,1,0:T(8,128)(2,1)}, u32[]{:S(2)}, u32[]{:S(2)}) %collective-permute-start.1) | collective-permute-done | bytes 393248 | tf_op jit(solution)/shard_map/ppermute | solution.py:77
  90.1 0.7 collective-permute-done.2
  90.8 0.0 copy-done.2
  90.8 2.7 %fusion.20 = f32[6,8,5,8,128]{4,3,2,1,0:T(8,128)S(1)} fusion(bf16[512,4,512]{2,0,1:T(8,128)(2,1)S(1)} %select_bitcast_fusion, bf16[1,6,64,512]{3,2,0,1:T(8,128)(2,1)} %bitcast.15, bf16[1,6,64,512]{3,2,0,1:T(8,128)(2,1)} %bitcast.12, bf16[1,6,64,512]{3,2,0,1:T(8,128)(2,1)} %bitcast.8, bf16[1,6,64,512]{3,2,0,1:T(8,128)(2,1)S(1)} %copy-done.2), kind=kOutput, calls=%fused_computation.32 | convolution fusion | flops 1008992256 | bytes 4653056 | tf_op jit(solution)/shard_map/dot_general | solution.py:79
  93.4 0.0 copy-done
  93.5 0.0 copy-start.1
  93.5 0.1 copy.91
  93.6 0.7 gather_fusion.5
  94.3 0.1 broadcast_multiply_fusion.1
  94.4 4.1 %collective-permute-done.5 = bf16[6,64,512]{2,1,0:T(8,128)(2,1)} collective-permute-done((bf16[6,64,512]{2,1,0:T(8,128)(2,1)}, bf16[6,64,512]{2,1,0:T(8,128)(2,1)}, u32[]{:S(2)}, u32[]{:S(2)}) %collective-permute-start.5) | collective-permute-done | bytes 393248 | tf_op jit(solution)/shard_map/ppermute | solution.py:77
  98.5 7.3 %collective-permute-done.6 = bf16[6,64,512]{2,1,0:T(8,128)(2,1)} collective-permute-done((bf16[6,64,512]{2,1,0:T(8,128)(2,1)}, bf16[6,64,512]{2,1,0:T(8,128)(2,1)}, u32[]{:S(2)}, u32[]{:S(2)}) %collective-permute-start.6) | collective-permute-done | bytes 393248 | tf_op jit(solution)/shard_map/ppermute | solution.py:77
  105.8 1.7 %collective-permute-done.7 = bf16[6,64,512]{2,1,0:T(8,128)(2,1)} collective-permute-done((bf16[6,64,512]{2,1,0:T(8,128)(2,1)S(1)}, bf16[6,64,512]{2,1,0:T(8,128)(2,1)}, u32[]{:S(2)}, u32[]{:S(2)}) %collective-permute-start.7) | collective-permute-done | bytes 393248 | tf_op jit(solution)/shard_map/ppermute | solution.py:77
  107.5 0.0 copy-done.1
  107.5 3.4 %fusion.25 = f32[6,8,5,8,128]{4,3,2,1,0:T(8,128)S(1)} fusion(bf16[512,4,512]{2,0,1:T(8,128)(2,1)} %copy-done, bf16[1,6,64,512]{3,2,1,0:T(8,128)(2,1)} %bitcast.40, bf16[1,6,64,512]{3,2,1,0:T(8,128)(2,1)} %bitcast.38, bf16[1,6,64,512]{3,2,1,0:T(8,128)(2,1)} %bitcast.36, bf16[1,6,64,512]{3,2,1,0:T(8,128)(2,1)S(1)} %copy-done.1), kind=kOutput, calls=%fused_computation.33 | convolution fusion | flops 1008992256 | bytes 4653056 | tf_op jit(solution)/shard_map/dot_general | solution.py:79
  110.9 0.1 copy.90
  111.1 0.7 gather_fusion.10
  111.8 0.8 dynamic-slice_bitcast_fusion.1
  112.5 0.0 collective-permute-start.3
  112.6 0.1 broadcast_multiply_fusion
  112.7 0.6 collective-permute-start.8
  113.3 1.2 collective-permute-done.3
  114.6 0.6 collective-permute-start.4
  115.2 0.0 collective-permute-done.8
  115.2 0.1 bitcast_add_fusion
  115.2 1.6 %collective-permute-start.9 = (f32[6,64,128]{2,1,0:T(8,128)S(1)}, f32[6,64,128]{2,1,0:T(8,128)S(1)}, u32[]{:S(2)}, u32[]{:S(2)}) collective-permute-start(f32[6,64,128]{2,1,0:T(8,128)S(1)} %dynamic-slice_bitcast_fusion.2), channel_id=1, source_target_pairs={{0,2},{2,0},{1,3},{3,1},{4,6},{6,4},{5,7},{7,5},{8,10},{10,8},{9,1... | collective-permute-start | bytes 589832 | tf_op jit(solution)/shard_map/ppermute | solution.py:24
  116.8 5.6 %collective-permute-done.4 = f32[6,64,128]{2,1,0:T(8,128)S(1)} collective-permute-done((f32[6,64,128]{2,1,0:T(8,128)S(1)}, f32[6,64,128]{2,1,0:T(8,128)S(1)}, u32[]{:S(2)}, u32[]{:S(2)}) %collective-permute-start.4) | collective-permute-done | bytes 196640 | tf_op jit(solution)/shard_map/ppermute | solution.py:24
  122.4 3.4 %collective-permute-done.9 = f32[6,64,128]{2,1,0:T(8,128)S(1)} collective-permute-done((f32[6,64,128]{2,1,0:T(8,128)S(1)}, f32[6,64,128]{2,1,0:T(8,128)S(1)}, u32[]{:S(2)}, u32[]{:S(2)}) %collective-permute-start.9) | collective-permute-done | bytes 196640 | tf_op jit(solution)/shard_map/ppermute | solution.py:24
  125.8 0.8 pad_maximum_fusion
  (14 shorter events, 0.3 us)
Async XLA Ops:
  9.8 8.9 %copy-start.3 = (s32[4,6]{1,0:T(4,128)S(1)}, s32[4,6]{1,0:T(4,128)}, u32[]{:S(2)}) copy-start(s32[4,6]{1,0:T(4,128)} %param.10) | copy-start | bytes 292
  34.7 10.2 %copy-start.4 = (s32[1,2]{1,0:T(1,128)S(1)}, s32[1,2]{1,0:T(1,128)}, u32[]{:S(2)}) copy-start(s32[1,2]{1,0:T(1,128)} %param.13) | copy-start | bytes 28
  36.5 33.0 %collective-permute-start = (bf16[6,64,512]{2,1,0:T(8,128)(2,1)}, bf16[6,64,512]{2,1,0:T(8,128)(2,1)}, u32[]{:S(2)}, u32[]{:S(2)}) collective-permute-start(bf16[6,64,512]{2,1,0:T(8,128)(2,1)} %get-tuple-element.15), channel_id=1, source_target_pairs={{0,4},{4,8},{8,12},{12,0},{1,5},{5,9},{9,13},{13,1},{2,6},{6,10},{... | collective-permute-start | bytes 1179656 | tf_op jit(solution)/shard_map/ppermute | solution.py:77
  38.1 52.0 %collective-permute-start.1 = (bf16[6,64,512]{2,1,0:T(8,128)(2,1)}, bf16[6,64,512]{2,1,0:T(8,128)(2,1)}, u32[]{:S(2)}, u32[]{:S(2)}) collective-permute-start(bf16[6,64,512]{2,1,0:T(8,128)(2,1)} %get-tuple-element.16), channel_id=1, source_target_pairs={{0,8},{4,12},{8,0},{12,4},{1,9},{5,13},{9,1},{13,5},{2,10},{6,14},... | collective-permute-start | bytes 1179656 | tf_op jit(solution)/shard_map/ppermute | solution.py:77
  39.3 51.5 %collective-permute-start.2 = (bf16[6,64,512]{2,1,0:T(8,128)(2,1)}, bf16[6,64,512]{2,1,0:T(8,128)(2,1)}, u32[]{:S(2)}, u32[]{:S(2)}) collective-permute-start(bf16[6,64,512]{2,1,0:T(8,128)(2,1)} %get-tuple-element.17), channel_id=1, source_target_pairs={{0,12},{4,0},{8,4},{12,8},{1,13},{5,1},{9,5},{13,9},{2,14},{6,2},{... | collective-permute-start | bytes 1179656 | tf_op jit(solution)/shard_map/ppermute | solution.py:77
  41.1 57.4 %collective-permute-start.5 = (bf16[6,64,512]{2,1,0:T(8,128)(2,1)}, bf16[6,64,512]{2,1,0:T(8,128)(2,1)}, u32[]{:S(2)}, u32[]{:S(2)}) collective-permute-start(bf16[6,64,512]{2,1,0:T(8,128)(2,1)} %get-tuple-element.18), channel_id=1, source_target_pairs={{0,4},{4,8},{8,12},{12,0},{1,5},{5,9},{9,13},{13,1},{2,6},{6,10},{... | collective-permute-start | bytes 1179656 | tf_op jit(solution)/shard_map/ppermute | solution.py:77
  41.3 64.5 %collective-permute-start.6 = (bf16[6,64,512]{2,1,0:T(8,128)(2,1)}, bf16[6,64,512]{2,1,0:T(8,128)(2,1)}, u32[]{:S(2)}, u32[]{:S(2)}) collective-permute-start(bf16[6,64,512]{2,1,0:T(8,128)(2,1)} %get-tuple-element.19), channel_id=1, source_target_pairs={{0,8},{4,12},{8,0},{12,4},{1,9},{5,13},{9,1},{13,5},{2,10},{6,14},... | collective-permute-start | bytes 1179656 | tf_op jit(solution)/shard_map/ppermute | solution.py:77
  64.3 2.0 %copy-start.5 = (s32[1,24]{1,0:T(1,128)S(1)}, s32[1,24]{1,0:T(1,128)}, u32[]{:S(2)}) copy-start(s32[1,24]{1,0:T(1,128)} %param.12) | copy-start | bytes 292
  64.3 2.0 %copy-start.6 = (s32[1,24]{1,0:T(1,128)S(1)}, s32[1,24]{1,0:T(1,128)}, u32[]{:S(2)}) copy-start(s32[1,24]{1,0:T(1,128)} %param.11) | copy-start | bytes 292
  67.6 23.2 %copy-start.2 = (bf16[1,6,64,512]{3,2,0,1:T(8,128)(2,1)S(1)}, bf16[1,6,64,512]{3,2,0,1:T(8,128)(2,1)}, u32[]{:S(2)}) copy-start(bf16[1,6,64,512]{3,2,0,1:T(8,128)(2,1)} %get-tuple-element.13) | copy-start | bytes 1179652
  69.5 24.0 %copy-start = (bf16[512,4,512]{2,0,1:T(8,128)(2,1)}, bf16[512,4,512]{2,0,1:T(8,128)(2,1)S(1)}, u32[]{:S(2)}) copy-start(bf16[512,4,512]{2,0,1:T(8,128)(2,1)S(1)} %select_bitcast_fusion) | copy-start | bytes 6291460
  69.5 38.0 %collective-permute-start.7 = (bf16[6,64,512]{2,1,0:T(8,128)(2,1)S(1)}, bf16[6,64,512]{2,1,0:T(8,128)(2,1)}, u32[]{:S(2)}, u32[]{:S(2)}) collective-permute-start(bf16[6,64,512]{2,1,0:T(8,128)(2,1)S(1)} %get-tuple-element.20), channel_id=1, source_target_pairs={{0,12},{4,0},{8,4},{12,8},{1,13},{5,1},{9,5},{13,9},{2,14},{6,2},{... | collective-permute-start | bytes 1179656 | tf_op jit(solution)/shard_map/ppermute | solution.py:77
  93.5 14.1 %copy-start.1 = (bf16[1,6,64,512]{3,2,1,0:T(8,128)(2,1)S(1)}, bf16[1,6,64,512]{3,2,1,0:T(8,128)(2,1)}, u32[]{:S(2)}) copy-start(bf16[1,6,64,512]{3,2,1,0:T(8,128)(2,1)} %get-tuple-element.14) | copy-start | bytes 1179652
  112.5 1.9 %collective-permute-start.3 = (f32[2,6,64,128]{3,2,1,0:T(8,128)}, f32[2,6,64,128]{3,2,1,0:T(8,128)S(1)}, u32[]{:S(2)}, u32[]{:S(2)}) collective-permute-start(f32[2,6,64,128]{3,2,1,0:T(8,128)} %dynamic-slice_bitcast_fusion.1), channel_id=1, source_target_pairs={{0,1},{1,0},{2,3},{3,2},{4,5},{5,4},{6,7},{7,6},{8,9},{9,8},{10,11... | collective-permute-start | bytes 1179656 | tf_op jit(solution)/shard_map/ppermute | solution.py:24
  112.7 2.5 %collective-permute-start.8 = (f32[2,6,64,128]{3,2,1,0:T(8,128)S(1)}, f32[2,6,64,128]{3,2,1,0:T(8,128)S(1)}, u32[]{:S(2)}, u32[]{:S(2)}) collective-permute-start(f32[2,6,64,128]{3,2,1,0:T(8,128)S(1)} %dynamic-slice_bitcast_fusion), channel_id=1, source_target_pairs={{0,1},{1,0},{2,3},{3,2},{4,5},{5,4},{6,7},{7,6},{8,9},{9,8},{10,11... | collective-permute-start | bytes 1179656 | tf_op jit(solution)/shard_map/ppermute | solution.py:24
  114.6 7.8 %collective-permute-start.4 = (f32[6,64,128]{2,1,0:T(8,128)S(1)}, f32[6,64,128]{2,1,0:T(8,128)S(1)}, u32[]{:S(2)}, u32[]{:S(2)}) collective-permute-start(f32[6,64,128]{2,1,0:T(8,128)S(1)} %dynamic-slice_bitcast_fusion.3), channel_id=1, source_target_pairs={{0,2},{2,0},{1,3},{3,1},{4,6},{6,4},{5,7},{7,5},{8,10},{10,8},{9,1... | collective-permute-start | bytes 589832 | tf_op jit(solution)/shard_map/ppermute | solution.py:24
  115.2 10.5 %collective-permute-start.9 = (f32[6,64,128]{2,1,0:T(8,128)S(1)}, f32[6,64,128]{2,1,0:T(8,128)S(1)}, u32[]{:S(2)}, u32[]{:S(2)}) collective-permute-start(f32[6,64,128]{2,1,0:T(8,128)S(1)} %dynamic-slice_bitcast_fusion.2), channel_id=1, source_target_pairs={{0,2},{2,0},{1,3},{3,1},{4,6},{6,4},{5,7},{7,5},{8,10},{10,8},{9,1... | collective-permute-start | bytes 589832 | tf_op jit(solution)/shard_map/ppermute | solution.py:24
